TPU v7x, 256 devices: a whole 4x4x8 slice. The times are simulated.
256 devices in a mesh: zone: 8 (over x, z_lo), brick: 32 (over z_hi, y, core).
Axes of the slice: x: 4, y: 4, z: 8 (z_hi: 4, z_lo: 2; z = z_hi * 2 + z_lo), core: 2. Of those that a mesh axis runs over, the one named last changes fastest.
Arguments:
- velocity: float32 [3, 2048, 64, 256], P(None, ('zone', 'brick')), may hold values from -3 to 3
- enthalpy: float32 [2048, 64, 256], P(('zone', 'brick')), may hold values from -6 to 6
- solvent: float32 [2048, 64, 256], P(('zone', 'brick')), may hold values from 0 to 1
- pressure: float32 [2048, 64, 256], P(('zone', 'brick')), may hold values from -6 to 6
- porosity: float32 [2048, 64, 256], P(('zone', 'brick')), may hold values from 0.1 to 1
- solid_mask: int32 [2048, 64, 256], P(('zone', 'brick')), may hold values 0 or 1
- nozzle_mask: int32 [2048, 256], P(('zone', 'brick')), may hold values 0 or 1
- zone_sizes: int32 [8], replicated, may hold values from 16 to 64, as said below
- zone_setpoint: float32 [8], replicated, may hold values from 0.5 to 2
- duct_source: int32 [256], P(('zone', 'brick')), may hold values from 0 to 7
- duct_span: int32 [256, 2], P(('zone', 'brick')), may hold values from 0 to 256, as said below
Outputs:
- velocity_new: float32 [3, 2048, 64, 256], P(None, ('zone', 'brick'))
- enthalpy_new: float32 [2048, 64, 256], P(('zone', 'brick'))
- solvent_new: float32 [2048, 64, 256], P(('zone', 'brick'))
- pressure_new: float32 [2048, 64, 256], P(('zone', 'brick'))
Inputs may be any that keep to these rules, and one draw needn't show every extreme that they name: `zone_sizes`: each zone's group holds a multiple of one thirty-second of all devices; the groups cover all devices, zone 0 first. duct_span[d,0] + duct_span[d,1] <= 256; duct_span[d,1] >= 64.
All inputs are finite; a program needn't handle non-finite values. No bound on the sum of `solid_mask` or of `nozzle_mask` on one device may be relied on, other than what follows from the above.
Results may differ from a plain program's by a relative error of at most 0.0003.
Values sent between devices are 32-bit elements; how exact they have to be, the bound alone decides.
No kernel may reach another device: no remote copies, remote signals or barrier semaphores. Data moves between devices by JAX's collectives and lax.ppermute only.
A program may use at most 128 MiB of HBM per device.

v0:
```python
import jax
import jax.numpy as jnp
from jax import lax
from jax.sharding import PartitionSpec as P

ITERS = 4
time_step = 0.2
viscosity = 0.1
diffusivity = 0.1
buoyancy = 0.5
evaporation = 0.5
latent_heat = 0.8
solvent_limit = 0.2


def extended(cells, sides, width):
    for axis, dim in sides:
        count = lax.axis_size(axis)
        ends = count - 1
        head = lax.slice_in_dim(cells, 0, width, axis=dim)
        tail = lax.slice_in_dim(cells, cells.shape[dim] - width, cells.shape[dim], axis=dim)
        cells = jnp.concatenate(
            [
                lax.ppermute(tail, axis, [(i, (i + 1) % count) for i in range(ends)]),
                cells,
                lax.ppermute(head, axis, [((i + 1) % count, i) for i in range(ends)]),
            ],
            axis=dim,
        )
    return cells


def shifted_down(values, axis):
    border = jnp.zeros_like(lax.slice_in_dim(values, 0, 1, axis=axis))
    inner = lax.slice_in_dim(values, 0, values.shape[axis] - 1, axis=axis)
    return jnp.concatenate([border, inner], axis=axis)


def shifted_up(values, axis):
    border = jnp.zeros_like(lax.slice_in_dim(values, 0, 1, axis=axis))
    inner = lax.slice_in_dim(values, 1, values.shape[axis], axis=axis)
    return jnp.concatenate([inner, border], axis=axis)


def momentum(vel_ext, pres_ext, heat_ext, poro_ext, components):
    open_here = poro_ext[1:-1]
    pressure_mid = pres_ext[1:-1]
    parts = []
    for component in components:
        values = vel_ext[component]
        centre = values[1:-1]
        laplacian = values[:-2] + values[2:] + shifted_down(centre, 1) + shifted_up(centre, 1)
        laplacian = laplacian + shifted_down(centre, 2) + shifted_up(centre, 2) - 6.0 * centre
        if component == 0:
            gradient = 0.5 * (pres_ext[2:] - pres_ext[:-2])
        else:
            gradient = 0.5 * (
                shifted_up(pressure_mid, component) - shifted_down(pressure_mid, component)
            )
        forcing = viscosity * laplacian - gradient
        if component == 1:
            forcing = forcing + buoyancy * heat_ext[1:-1]
        parts.append(open_here * (centre + time_step * forcing))
    return jnp.stack(parts)


def divergence_parts(first_ext, vel_star):
    result = 0.5 * (first_ext[2:] - first_ext[:-2])
    middle = vel_star[1]
    result = result + 0.5 * (shifted_up(middle, 1) - shifted_down(middle, 1))
    across = vel_star[2]
    return result + 0.5 * (shifted_up(across, 2) - shifted_down(across, 2))


def transport(scalar_ext, vel_star):
    centre = scalar_ext[1:-1]
    laplacian = scalar_ext[:-2] + scalar_ext[2:] + shifted_down(centre, 1) + shifted_up(centre, 1)
    laplacian = laplacian + shifted_down(centre, 2) + shifted_up(centre, 2) - 6.0 * centre
    advect = jnp.maximum(vel_star[0], 0.0) * (centre - scalar_ext[:-2]) + jnp.minimum(
        vel_star[0], 0.0
    ) * (scalar_ext[2:] - centre)
    for component in (1, 2):
        advect = advect + jnp.maximum(vel_star[component], 0.0) * (
            centre - shifted_down(centre, component)
        )
        advect = advect + jnp.minimum(vel_star[component], 0.0) * (
            shifted_up(centre, component) - centre
        )
    return centre + time_step * (diffusivity * laplacian - advect)


def sweep(pres_ext, open_ext, source):
    open_here = open_ext[1:-1]
    pressure_mid = pres_ext[1:-1]
    face_back = 0.5 * (open_here + open_ext[:-2])
    face_front = 0.5 * (open_here + open_ext[2:])
    numerator = face_back * pres_ext[:-2] + face_front * pres_ext[2:] - source
    denominator = face_back + face_front
    for component in (1, 2):
        face_low = 0.5 * (open_here + shifted_down(open_here, component))
        face_high = 0.5 * (open_here + shifted_up(open_here, component))
        numerator = (
            numerator
            + face_low * shifted_down(pressure_mid, component)
            + face_high * shifted_up(pressure_mid, component)
        )
        denominator = denominator + face_low + face_high
    inside = open_here > 0.0
    return jnp.where(inside, numerator / jnp.where(inside, denominator, 1.0), 0.0)


def on_device(
    velocity,
    enthalpy,
    solvent,
    pressure,
    porosity,
    solid_mask,
    nozzle_mask,
    zone_sizes,
    zone_setpoint,
    duct_source,
    duct_span,
):
    stacked = jnp.concatenate(
        [velocity, jnp.stack([enthalpy, solvent, pressure, porosity])], axis=0
    )
    padded = extended(stacked, ((("zone", "brick"), 1),), 1)
    heat_ext = padded[3]
    solv_ext = padded[4]
    poro_ext = padded[6]
    vel_star = momentum(padded[0:3], padded[5], padded[3], padded[6], (0, 1, 2))
    first_ext = extended(vel_star[0], ((("zone", "brick"), 0),), 1)
    source = divergence_parts(first_ext, vel_star) / time_step
    heat_new = transport(heat_ext, vel_star)
    solv_new = transport(solv_ext, vel_star)
    drying = time_step * evaporation * solid_mask.astype(jnp.float32) * solvent
    heat_new = heat_new - latent_heat * drying
    solv_new = solv_new - drying
    device = lax.axis_index(("zone", "brick"))
    starts = jnp.cumsum(zone_sizes) - zone_sizes
    zone_here = jnp.sum((device >= starts).astype(jnp.int32)) - 1
    choose = (jnp.arange(zone_sizes.shape[0], dtype=jnp.int32) == zone_here).astype(jnp.float32)
    totals = lax.psum(choose * jnp.sum(solvent[:, -1, :]), ("zone", "brick"))
    counts = zone_sizes.astype(jnp.float32) * (enthalpy.shape[0] * enthalpy.shape[2])
    means = totals / counts
    fresh_all = means / (means + solvent_limit)
    fresh = jnp.sum(choose * fresh_all)
    target = jnp.sum(choose * zone_setpoint)
    planes = jnp.stack([enthalpy[:, -1, :], solvent[:, -1, :]])[None]
    gathered = lax.all_gather(planes, "zone", axis=0, tiled=True)
    pick = (jnp.arange(gathered.shape[0], dtype=jnp.int32) == duct_source[0]).astype(jnp.float32)
    arrived = jnp.sum(pick[:, None, None, None] * gathered, axis=0)
    supply_heat = (1.0 - fresh) * arrived[0] + fresh * target
    supply_solv = (1.0 - fresh) * arrived[1]
    column = jnp.arange(enthalpy.shape[2], dtype=jnp.int32)
    inside_box = (column >= duct_span[0, 0]) & (column < duct_span[0, 0] + duct_span[0, 1])
    jets = (nozzle_mask > 0) & inside_box[None, :]
    heat_layer = jnp.where(jets, supply_heat, heat_new[:, 0, :])
    solv_layer = jnp.where(jets, supply_solv, solv_new[:, 0, :])
    enthalpy_new = jnp.concatenate([heat_layer[:, None, :], heat_new[:, 1:, :]], axis=1)
    solvent_new = jnp.concatenate([solv_layer[:, None, :], solv_new[:, 1:, :]], axis=1)
    iterate = pressure
    for iteration in range(ITERS):
        pres_ext = extended(iterate, ((("zone", "brick"), 0),), 1)
        iterate = sweep(pres_ext, poro_ext, source)
    pres_ext = extended(iterate, ((("zone", "brick"), 0),), 1)
    gradients = jnp.stack(
        [
            0.5 * (pres_ext[2:] - pres_ext[:-2]),
            0.5 * (shifted_up(iterate, 1) - shifted_down(iterate, 1)),
            0.5 * (shifted_up(iterate, 2) - shifted_down(iterate, 2)),
        ]
    )
    velocity_new = vel_star - time_step * porosity[None] * gradients
    return (velocity_new, enthalpy_new, solvent_new, iterate)


def solution(mesh):
    placed = (
        P(None, ("zone", "brick"), None, None),
        P(("zone", "brick"), None, None),
        P(("zone", "brick"), None, None),
        P(("zone", "brick"), None, None),
        P(("zone", "brick"), None, None),
        P(("zone", "brick"), None, None),
        P(("zone", "brick"), None),
        P(),
        P(),
        P(("zone", "brick")),
        P(("zone", "brick"), None),
    )
    return jax.shard_map(
        on_device,
        mesh=mesh,
        in_specs=placed,
        out_specs=(
            P(None, ("zone", "brick"), None, None),
            P(("zone", "brick"), None, None),
            P(("zone", "brick"), None, None),
            P(("zone", "brick"), None, None),
        ),
        check_vma=False,
    )
```

profile of v0, /device:TPU:32, one launch (start us, length us, event | category | flops | bytes accessed | tf_op | source)
XLA Modules:
  0.0 256.3 jit_solution(2717288666460999411)
XLA Ops:
  0.7 2.4 fusion.106
  4.8 1.9 fusion.105
  6.7 1.9 collective-permute-start
  8.6 9.6 %collective-permute-start.1 = (f32[7,1,64,256]{3,1,2,0:T(1,128)}, f32[7,1,64,256]{3,1,2,0:T(1,128)}, u32[]{:S(2)}, u32[]{:S(2)}) collective-permute-start(f32[7,1,64,256]{3,1,2,0:T(1,128)} %get-tuple-element.31), channel_id=1, source_target_pairs={{1,0},{2,1},{3,2},{4,3},{5,4},{6,5},{7,6},{8,7},{9,8},{10,9},{11,1... | collective-permute-start | bytes 1376264 | tf_op jit(solution)/shard_map/ppermute | solution.py:26
  18.3 1.9 collective-permute-start.2
  20.3 8.8 %collective-permute-start.3 = (f32[1,64,256]{2,0,1:T(1,128)S(1)}, f32[1,64,256]{2,0,1:T(1,128)S(1)}, u32[]{:S(2)}, u32[]{:S(2)}) collective-permute-start(f32[1,64,256]{2,0,1:T(1,128)S(1)} %copy.188), channel_id=1, source_target_pairs={{1,0},{2,1},{3,2},{4,3},{5,4},{6,5},{7,6},{8,7},{9,8},{10,9},{11,1... | collective-permute-start | bytes 196616 | tf_op jit(solution)/shard_map/ppermute | solution.py:26
  29.2 1.7 fusion.128
  30.9 1.5 fusion.127
  45.2 74.0 %psum.7 = f32[8]{0:T(128)S(1)} all-reduce(f32[8]{0:T(128)S(1)} %fusion.98), channel_id=1, replica_groups=mesh['zone'=8,'brick'=32] {'zone','brick'}, use_global_device_ids=true, to_apply=%region_3.4 | all-reduce | flops 8 | bytes 64 | tf_op jit(solution)/shard_map/psum | solution.py:144
  119.9 26.4 %all-gather = f32[16,8,256]{2,1,0:T(8,128)S(1)} all-gather(f32[2,8,256]{2,1,0:T(8,128)S(1)} %pad_maximum_fusion.16), channel_id=2, replica_groups=mesh['zone'=8,'brick'=32] {'zone'}, dimensions={0}, use_global_device_ids=true | all-gather | bytes 147456 | tf_op jit(solution)/shard_map/all_gather | solution.py:151
  153.0 2.2 copy.269
  155.2 2.2 copy.270
  161.7 1.7 fusion.134
  164.2 6.4 %add_subtract_fusion = (f32[8,64,256]{2,0,1:T(8,128)S(1)}, f32[8,64,256]{2,0,1:T(8,128)S(1)}, f32[8,64,256]{2,0,1:T(8,128)S(1)}, f32[8,64,256]{2,0,1:T(8,128)S(1)}) fusion(f32[8,64,255]{2,0,1:T(8,128)S(1)} %get-tuple-element.108, f32[8,64,255]{2,0,1:T(8,128)S(1)} %get-tuple-element.109, f32[8,63,256]{2,0,1:T(8,128)} %get-tuple-element.106, ...), kind=kLoop, calls=%fused_computation.125 | loop fusion | flops 12058624 | bytes 20738048 | tf_op jit(solution)/shard_map/sub | solution.py:139
  173.6 2.6 %multiply_subtract_fusion = f32[8,64,256]{2,0,1:T(8,128)S(1)} fusion(f32[8,64,255]{2,0,1:T(8,128)S(1)} %copy-done.18, f32[8,64,255]{2,0,1:T(8,128)S(1)} %copy-done.17, f32[8,63,256]{2,0,1:T(8,128)S(1)} %copy-done.22, f32[8,63,256]{2,0,1:T(8,128)S(1)} %copy-done.21, f32[7,8,64,256]{3,1,2,0:T(8,128)S(1)} %copy-done.1, ...), kind=kLoop, calls=%fused_computation.126 | loop fusion | flops 5373952 | bytes 10334208 | tf_op jit(solution)/shard_map/sub | solution.py:138
  176.3 2.2 collective-permute-start.4
  178.5 2.4 collective-permute-start.5
  181.9 8.0 %collective-permute-done.5 = f32[1,64,256]{2,0,1:T(1,128)S(1)} collective-permute-done((f32[1,64,256]{2,0,1:T(1,128)S(1)}, f32[1,64,256]{2,0,1:T(1,128)S(1)}, u32[]{:S(2)}, u32[]{:S(2)}) %collective-permute-start.5) | collective-permute-done | bytes 65568 | tf_op jit(solution)/shard_map/ppermute | solution.py:24
  189.9 2.5 fusion.47
  192.8 1.9 collective-permute-start.6
  194.7 8.8 %collective-permute-start.7 = (f32[1,64,256]{2,0,1:T(1,128)S(1)}, f32[1,64,256]{2,0,1:T(1,128)S(1)}, u32[]{:S(2)}, u32[]{:S(2)}) collective-permute-start(f32[1,64,256]{2,0,1:T(1,128)S(1)} %get-tuple-element.67), channel_id=1, source_target_pairs={{1,0},{2,1},{3,2},{4,3},{5,4},{6,5},{7,6},{8,7},{9,8},{10,9},{11,1... | collective-permute-start | bytes 196616 | tf_op jit(solution)/shard_map/ppermute | solution.py:26
  203.5 1.8 collective-permute-done.7
  206.3 1.9 collective-permute-start.8
  208.2 8.8 %collective-permute-start.9 = (f32[1,64,256]{2,0,1:T(1,128)S(1)}, f32[1,64,256]{2,0,1:T(1,128)S(1)}, u32[]{:S(2)}, u32[]{:S(2)}) collective-permute-start(f32[1,64,256]{2,0,1:T(1,128)S(1)} %get-tuple-element.61), channel_id=1, source_target_pairs={{1,0},{2,1},{3,2},{4,3},{5,4},{6,5},{7,6},{8,7},{9,8},{10,9},{11,1... | collective-permute-start | bytes 196616 | tf_op jit(solution)/shard_map/ppermute | solution.py:26
  217.1 1.8 collective-permute-done.9
  219.9 1.9 collective-permute-start.10
  221.8 9.0 %collective-permute-start.11 = (f32[1,64,256]{2,0,1:T(1,128)S(1)}, f32[1,64,256]{2,0,1:T(1,128)S(1)}, u32[]{:S(2)}, u32[]{:S(2)}) collective-permute-start(f32[1,64,256]{2,0,1:T(1,128)S(1)} %get-tuple-element.55), channel_id=1, source_target_pairs={{1,0},{2,1},{3,2},{4,3},{5,4},{6,5},{7,6},{8,7},{9,8},{10,9},{11,1... | collective-permute-start | bytes 196616 | tf_op jit(solution)/shard_map/ppermute | solution.py:26
  231.0 1.6 collective-permute-done.11
  234.6 8.8 %collective-permute-start.12 = (f32[1,64,256]{2,0,1:T(1,128)S(1)}, f32[1,64,256]{2,0,1:T(1,128)S(1)}, u32[]{:S(2)}, u32[]{:S(2)}) collective-permute-start(f32[1,64,256]{2,0,1:T(1,128)S(1)} %get-tuple-element.44), channel_id=1, source_target_pairs={{1,0},{2,1},{3,2},{4,3},{5,4},{6,5},{7,6},{8,7},{9,8},{10,9},{11,1... | collective-permute-start | bytes 196616 | tf_op jit(solution)/shard_map/ppermute | solution.py:26
  243.4 1.9 collective-permute-start.13
  245.6 8.5 %collective-permute-done.13 = f32[1,64,256]{2,0,1:T(1,128)S(1)} collective-permute-done((f32[1,64,256]{2,0,1:T(1,128)S(1)}, f32[1,64,256]{2,0,1:T(1,128)S(1)}, u32[]{:S(2)}, u32[]{:S(2)}) %collective-permute-start.13) | collective-permute-done | bytes 65568 | tf_op jit(solution)/shard_map/ppermute | solution.py:24
  254.6 1.6 copy.229
  (128 shorter events, 31.8 us)
Async XLA Ops:
  0.6 2.4 copy-start.6
  0.6 2.8 %copy-start.4 = (f32[8,64,256]{2,1,0:T(8,128)S(1)}, f32[8,64,256]{2,1,0:T(8,128)}, u32[]{:S(2)}) copy-start(f32[8,64,256]{2,1,0:T(8,128)} %param.13) | copy-start | bytes 1572868
  4.7 24.5 %copy-start = (f32[7,8,64,256]{3,1,2,0:T(8,128)}, f32[7,8,64,256]{3,1,2,0:T(8,128)S(1)}, u32[]{:S(2)}) copy-start(f32[7,8,64,256]{3,1,2,0:T(8,128)S(1)} %bitcast_dynamic-update-slice_fusion) | copy-start | bytes 11010052
  6.7 156.8 %collective-permute-start = (f32[7,1,64,256]{3,1,2,0:T(1,128)}, f32[7,1,64,256]{3,1,2,0:T(1,128)}, u32[]{:S(2)}, u32[]{:S(2)}) collective-permute-start(f32[7,1,64,256]{3,1,2,0:T(1,128)} %get-tuple-element.32), channel_id=1, source_target_pairs={{0,1},{1,2},{2,3},{3,4},{4,5},{5,6},{6,7},{7,8},{8,9},{9,10},{10,1... | collective-permute-start | bytes 1376264 | tf_op jit(solution)/shard_map/ppermute | solution.py:24
  8.6 154.8 %collective-permute-start.1 = (f32[7,1,64,256]{3,1,2,0:T(1,128)}, f32[7,1,64,256]{3,1,2,0:T(1,128)}, u32[]{:S(2)}, u32[]{:S(2)}) collective-permute-start(f32[7,1,64,256]{3,1,2,0:T(1,128)} %get-tuple-element.31), channel_id=1, source_target_pairs={{1,0},{2,1},{3,2},{4,3},{5,4},{6,5},{7,6},{8,7},{9,8},{10,9},{11,1... | collective-permute-start | bytes 1376264 | tf_op jit(solution)/shard_map/ppermute | solution.py:26
  18.3 163.6 %collective-permute-start.2 = (f32[1,64,256]{2,0,1:T(1,128)S(1)}, f32[1,64,256]{2,0,1:T(1,128)S(1)}, u32[]{:S(2)}, u32[]{:S(2)}) collective-permute-start(f32[1,64,256]{2,0,1:T(1,128)S(1)} %copy.185), channel_id=1, source_target_pairs={{0,1},{1,2},{2,3},{3,4},{4,5},{5,6},{6,7},{7,8},{8,9},{9,10},{10,1... | collective-permute-start | bytes 196616 | tf_op jit(solution)/shard_map/ppermute | solution.py:24
  20.3 161.6 %collective-permute-start.3 = (f32[1,64,256]{2,0,1:T(1,128)S(1)}, f32[1,64,256]{2,0,1:T(1,128)S(1)}, u32[]{:S(2)}, u32[]{:S(2)}) collective-permute-start(f32[1,64,256]{2,0,1:T(1,128)S(1)} %copy.188), channel_id=1, source_target_pairs={{1,0},{2,1},{3,2},{4,3},{5,4},{6,5},{7,6},{8,7},{9,8},{10,9},{11,1... | collective-permute-start | bytes 196616 | tf_op jit(solution)/shard_map/ppermute | solution.py:26
  29.2 11.4 %copy-start.3 = (f32[8,64,256]{2,0,1:T(8,128)}, f32[8,64,256]{2,0,1:T(8,128)S(1)}, u32[]{:S(2)}) copy-start(f32[8,64,256]{2,0,1:T(8,128)S(1)} %get-tuple-element.35) | copy-start | bytes 1572868
  153.0 4.4 %copy-start.20 = (f32[8,63,256]{2,1,0:T(8,128)S(1)}, f32[8,63,256]{2,1,0:T(8,128)}, u32[]{:S(2)}) copy-start(f32[8,63,256]{2,1,0:T(8,128)} %get-tuple-element.76) | copy-start | bytes 1548292
  153.0 5.5 %copy-start.19 = (f32[8,63,256]{2,1,0:T(8,128)S(1)}, f32[8,63,256]{2,1,0:T(8,128)}, u32[]{:S(2)}) copy-start(f32[8,63,256]{2,1,0:T(8,128)} %get-tuple-element.77) | copy-start | bytes 1548292
  161.7 2.4 copy-start.1
  161.7 2.5 copy-start.5
  164.2 6.5 %copy-start.25 = (s32[8,256]{1,0:T(8,128)S(1)}, s32[8,256]{1,0:T(8,128)}, u32[]{:S(2)}) copy-start(s32[8,256]{1,0:T(8,128)} %param.17) | copy-start | bytes 24580
  173.6 16.3 %copy-start.23 = (f32[8,63,256]{2,0,1:T(8,128)S(1)}, f32[8,63,256]{2,0,1:T(8,128)}, u32[]{:S(2)}) copy-start(f32[8,63,256]{2,0,1:T(8,128)} %copy.271) | copy-start | bytes 1548292
  173.6 16.3 %copy-start.24 = (f32[8,63,256]{2,0,1:T(8,128)S(1)}, f32[8,63,256]{2,0,1:T(8,128)}, u32[]{:S(2)}) copy-start(f32[8,63,256]{2,0,1:T(8,128)} %copy.272) | copy-start | bytes 1548292
  176.2 13.7 %copy-start.8 = (f32[8,64,255]{2,0,1:T(8,128)S(1)}, f32[8,64,255]{2,0,1:T(8,128)}, u32[]{:S(2)}) copy-start(f32[8,64,255]{2,0,1:T(8,128)} %get-tuple-element.84) | copy-start | bytes 1566724
  176.2 13.7 %copy-start.9 = (f32[8,64,255]{2,0,1:T(8,128)S(1)}, f32[8,64,255]{2,0,1:T(8,128)}, u32[]{:S(2)}) copy-start(f32[8,64,255]{2,0,1:T(8,128)} %get-tuple-element.85) | copy-start | bytes 1566724
  176.2 13.7 %copy-start.10 = (f32[8,63,256]{2,0,1:T(8,128)S(1)}, f32[8,63,256]{2,0,1:T(8,128)}, u32[]{:S(2)}) copy-start(f32[8,63,256]{2,0,1:T(8,128)} %get-tuple-element.90) | copy-start | bytes 1548292
  176.2 13.7 %copy-start.11 = (f32[8,63,256]{2,0,1:T(8,128)S(1)}, f32[8,63,256]{2,0,1:T(8,128)}, u32[]{:S(2)}) copy-start(f32[8,63,256]{2,0,1:T(8,128)} %get-tuple-element.91) | copy-start | bytes 1548292
  176.2 13.7 %copy-start.15 = (f32[8,64,255]{2,0,1:T(8,128)S(1)}, f32[8,64,255]{2,0,1:T(8,128)}, u32[]{:S(2)}) copy-start(f32[8,64,255]{2,0,1:T(8,128)} %copy.269) | copy-start | bytes 1566724
  176.2 13.7 %copy-start.16 = (f32[8,64,255]{2,0,1:T(8,128)S(1)}, f32[8,64,255]{2,0,1:T(8,128)}, u32[]{:S(2)}) copy-start(f32[8,64,255]{2,0,1:T(8,128)} %copy.270) | copy-start | bytes 1566724
  176.3 5.6 %collective-permute-start.4 = (f32[1,64,256]{2,0,1:T(1,128)S(1)}, f32[1,64,256]{2,0,1:T(1,128)S(1)}, u32[]{:S(2)}, u32[]{:S(2)}) collective-permute-start(f32[1,64,256]{2,0,1:T(1,128)S(1)} %get-tuple-element.68), channel_id=1, source_target_pairs={{1,0},{2,1},{3,2},{4,3},{5,4},{6,5},{7,6},{8,7},{9,8},{10,9},{11,1... | collective-permute-start | bytes 196616 | tf_op jit(solution)/shard_map/ppermute | solution.py:26
  178.5 11.4 %collective-permute-start.5 = (f32[1,64,256]{2,0,1:T(1,128)S(1)}, f32[1,64,256]{2,0,1:T(1,128)S(1)}, u32[]{:S(2)}, u32[]{:S(2)}) collective-permute-start(f32[1,64,256]{2,0,1:T(1,128)S(1)} %get-tuple-element.69), channel_id=1, source_target_pairs={{0,1},{1,2},{2,3},{3,4},{4,5},{5,6},{6,7},{7,8},{8,9},{9,10},{10,1... | collective-permute-start | bytes 196616 | tf_op jit(solution)/shard_map/ppermute | solution.py:24
  192.8 10.8 %collective-permute-start.6 = (f32[1,64,256]{2,0,1:T(1,128)S(1)}, f32[1,64,256]{2,0,1:T(1,128)S(1)}, u32[]{:S(2)}, u32[]{:S(2)}) collective-permute-start(f32[1,64,256]{2,0,1:T(1,128)S(1)} %get-tuple-element.66), channel_id=1, source_target_pairs={{0,1},{1,2},{2,3},{3,4},{4,5},{5,6},{6,7},{7,8},{8,9},{9,10},{10,1... | collective-permute-start | bytes 196616 | tf_op jit(solution)/shard_map/ppermute | solution.py:24
  194.7 10.7 %collective-permute-start.7 = (f32[1,64,256]{2,0,1:T(1,128)S(1)}, f32[1,64,256]{2,0,1:T(1,128)S(1)}, u32[]{:S(2)}, u32[]{:S(2)}) collective-permute-start(f32[1,64,256]{2,0,1:T(1,128)S(1)} %get-tuple-element.67), channel_id=1, source_target_pairs={{1,0},{2,1},{3,2},{4,3},{5,4},{6,5},{7,6},{8,7},{9,8},{10,9},{11,1... | collective-permute-start | bytes 196616 | tf_op jit(solution)/shard_map/ppermute | solution.py:26
  206.3 10.8 %collective-permute-start.8 = (f32[1,64,256]{2,0,1:T(1,128)S(1)}, f32[1,64,256]{2,0,1:T(1,128)S(1)}, u32[]{:S(2)}, u32[]{:S(2)}) collective-permute-start(f32[1,64,256]{2,0,1:T(1,128)S(1)} %get-tuple-element.60), channel_id=1, source_target_pairs={{0,1},{1,2},{2,3},{3,4},{4,5},{5,6},{6,7},{7,8},{8,9},{9,10},{10,1... | collective-permute-start | bytes 196616 | tf_op jit(solution)/shard_map/ppermute | solution.py:24
  208.2 10.7 %collective-permute-start.9 = (f32[1,64,256]{2,0,1:T(1,128)S(1)}, f32[1,64,256]{2,0,1:T(1,128)S(1)}, u32[]{:S(2)}, u32[]{:S(2)}) collective-permute-start(f32[1,64,256]{2,0,1:T(1,128)S(1)} %get-tuple-element.61), channel_id=1, source_target_pairs={{1,0},{2,1},{3,2},{4,3},{5,4},{6,5},{7,6},{8,7},{9,8},{10,9},{11,1... | collective-permute-start | bytes 196616 | tf_op jit(solution)/shard_map/ppermute | solution.py:26
  219.9 11.0 %collective-permute-start.10 = (f32[1,64,256]{2,0,1:T(1,128)S(1)}, f32[1,64,256]{2,0,1:T(1,128)S(1)}, u32[]{:S(2)}, u32[]{:S(2)}) collective-permute-start(f32[1,64,256]{2,0,1:T(1,128)S(1)} %get-tuple-element.54), channel_id=1, source_target_pairs={{0,1},{1,2},{2,3},{3,4},{4,5},{5,6},{6,7},{7,8},{8,9},{9,10},{10,1... | collective-permute-start | bytes 196616 | tf_op jit(solution)/shard_map/ppermute | solution.py:24
  221.8 10.7 %collective-permute-start.11 = (f32[1,64,256]{2,0,1:T(1,128)S(1)}, f32[1,64,256]{2,0,1:T(1,128)S(1)}, u32[]{:S(2)}, u32[]{:S(2)}) collective-permute-start(f32[1,64,256]{2,0,1:T(1,128)S(1)} %get-tuple-element.55), channel_id=1, source_target_pairs={{1,0},{2,1},{3,2},{4,3},{5,4},{6,5},{7,6},{8,7},{9,8},{10,9},{11,1... | collective-permute-start | bytes 196616 | tf_op jit(solution)/shard_map/ppermute | solution.py:26
  234.6 11.1 %collective-permute-start.12 = (f32[1,64,256]{2,0,1:T(1,128)S(1)}, f32[1,64,256]{2,0,1:T(1,128)S(1)}, u32[]{:S(2)}, u32[]{:S(2)}) collective-permute-start(f32[1,64,256]{2,0,1:T(1,128)S(1)} %get-tuple-element.44), channel_id=1, source_target_pairs={{1,0},{2,1},{3,2},{4,3},{5,4},{6,5},{7,6},{8,7},{9,8},{10,9},{11,1... | collective-permute-start | bytes 196616 | tf_op jit(solution)/shard_map/ppermute | solution.py:26
  243.4 10.7 %collective-permute-start.13 = (f32[1,64,256]{2,0,1:T(1,128)S(1)}, f32[1,64,256]{2,0,1:T(1,128)S(1)}, u32[]{:S(2)}, u32[]{:S(2)}) collective-permute-start(f32[1,64,256]{2,0,1:T(1,128)S(1)} %get-tuple-element.45), channel_id=1, source_target_pairs={{0,1},{1,2},{2,3},{3,4},{4,5},{5,6},{6,7},{7,8},{8,9},{9,10},{10,1... | collective-permute-start | bytes 196616 | tf_op jit(solution)/shard_map/ppermute | solution.py:24
  245.4 8.9 %copy-start.14 = (f32[8,64,256]{2,0,1:T(8,128)S(1)}, f32[8,64,256]{2,0,1:T(8,128)}, u32[]{:S(2)}) copy-start(f32[8,64,256]{2,0,1:T(8,128)} %broadcast_multiply_fusion) | copy-start | bytes 1572868
  (9 other events, 12.2 us)
where the time goes:
time: 257 us; the launch traced here: 256 us
  blocking collectives  100 us (39%)
  starting transfers between devices  69.9 us (27%)
  local copies, waits for them, and re-layouts  36.6 us (14%)
  other arithmetic  21.9 us (9%)
  waiting for transfers between devices  21.6 us (8%)
  between operations  5.9 us (2%)
    psum x1, blocking collectives, on_device(): totals = lax.psum(choose * jnp.sum(solvent[:, -1, :]), ('zone', 'brick'))  74 us
    ppermute x7, starting transfers between devices, extended(): lax.ppermute(head, axis, [((i + 1) % count, i) for i in range(ends)])  56 us
    all_gather x1, blocking collectives, on_device(): gathered = lax.all_gather(planes, 'zone', axis=0, tiled=True)  26.4 us
    unnamed x70, local copies, waits for them, and re-layouts  18.1 us
    ppermute x7, waiting for transfers between devices, extended(): lax.ppermute(tail, axis, [(i, (i + 1) % count) for i in range(ends)])  16.4 us
    ppermute x7, starting transfers between devices, extended(): lax.ppermute(tail, axis, [(i, (i + 1) % count) for i in range(ends)])  13.9 us
    slice x12, local copies, waits for them, and re-layouts, shifted_down(): inner = lax.slice_in_dim(values, 0, values.shape[axis] - 1, axis=axis)  9.19 us
    sub x1, other arithmetic, on_device(): solv_new = solv_new - drying  6.42 us
  transfers between devices with their start and end apart: 14, of which 5 were waited for; matrix products, arithmetic and copies ran while one was open for 16% of the time, Pallas kernels for 0%

commit v1 on v0

--- a/solution.py
+++ b/solution.py
@@ -1,3 +1,4 @@
+import functools
 import jax
 import jax.numpy as jnp
 from jax import lax
@@ -11,6 +12,17 @@
 evaporation = 0.5
 latent_heat = 0.8
 solvent_limit = 0.2
+
+
+def render_trails(my_data, group_axis, dim_i):
+    val2 = jax.lax.axis_size(group_axis)
+    y = jnp.stack([my_data] * val2, 0)
+    raw_out = jax.lax.all_to_all(y, group_axis, 0, 0)
+    arr_out = jnp.concatenate(raw_out, dim_i)
+    return arr_out
+
+
+_wait_map = functools.partial(render_trails, group_axis="zone", dim_i=0)
 
 
 def extended(cells, sides, width):
@@ -148,7 +160,7 @@
     fresh = jnp.sum(choose * fresh_all)
     target = jnp.sum(choose * zone_setpoint)
     planes = jnp.stack([enthalpy[:, -1, :], solvent[:, -1, :]])[None]
-    gathered = lax.all_gather(planes, "zone", axis=0, tiled=True)
+    gathered = _wait_map(planes)
     pick = (jnp.arange(gathered.shape[0], dtype=jnp.int32) == duct_source[0]).astype(jnp.float32)
     arrived = jnp.sum(pick[:, None, None, None] * gathered, axis=0)
     supply_heat = (1.0 - fresh) * arrived[0] + fresh * target

time: 257 us -> 249 us (0.969)
  blocking collectives: 100 us -> 74 us
  local copies, waits for them, and re-layouts: 36.6 us -> 46.6 us
  starting transfers between devices: 69.9 us -> 76.1 us
  other arithmetic: 21.9 us -> 25.3 us
    all_gather x1 -> x0, blocking collectives: 26.4 us -> none  [on_device(): gathered = lax.all_gather(planes, 'zone', axis=0, tiled=True)]
    unnamed x70 -> x100, local copies, waits for them, and re-layouts: 18.1 us -> 27.8 us
    add x0 -> x2, other arithmetic: none -> 7.21 us  [the longest x1 4.38 us: transport(): advect + jnp.maximum(vel_star[component], 0.0) * (centre - shifted_down(c...]
    all_to_all x0 -> x1, starting transfers between devices: none -> 5.76 us  [render_trails(): raw_out = jax.lax.all_to_all(y, group_axis, 0, 0)]
    sub x1, other arithmetic: 6.42 us -> 0.72 us  [on_device(): solv_new = solv_new - drying]
    slice x12 -> x13, local copies, waits for them, and re-layouts: 9.19 us -> 7.15 us  [shifted_down(): inner = lax.slice_in_dim(values, 0, values.shape[axis] - 1, axis=axis)]
  transfers between devices with their start and end apart: 14 -> 15, of which waited for: 5 -> 5; matrix products, arithmetic and copies ran while one was open for 16% -> 21% of each run, Pallas kernels for 0% -> 0%
where the time goes in v1:
time: 249 us; the launch traced here: 248 us
  starting transfers between devices  76.1 us (31%)
  blocking collectives  74 us (30%)
  local copies, waits for them, and re-layouts  46.6 us (19%)
  other arithmetic  25.3 us (10%)
  waiting for transfers between devices  20.3 us (8%)
  between operations  5.96 us (2%)
    psum x1, blocking collectives, on_device(): totals = lax.psum(choose * jnp.sum(solvent[:, -1, :]), ('zone', 'brick'))  74 us
    ppermute x7, starting transfers between devices, extended(): lax.ppermute(head, axis, [((i + 1) % count, i) for i in range(ends)])  56.7 us
    unnamed x100, local copies, waits for them, and re-layouts  27.8 us
    ppermute x7, waiting for transfers between devices, extended(): lax.ppermute(tail, axis, [(i, (i + 1) % count) for i in range(ends)])  14.9 us
    ppermute x7, starting transfers between devices, extended(): lax.ppermute(tail, axis, [(i, (i + 1) % count) for i in range(ends)])  13.7 us
    slice x13, local copies, waits for them, and re-layouts, shifted_down(): inner = lax.slice_in_dim(values, 0, values.shape[axis] - 1, axis=axis)  7.15 us
    all_to_all x1, starting transfers between devices, render_trails(): raw_out = jax.lax.all_to_all(y, group_axis, 0, 0)  5.76 us
    ppermute x7, waiting for transfers between devices, extended(): lax.ppermute(head, axis, [((i + 1) % count, i) for i in range(ends)])  5.4 us
  transfers between devices with their start and end apart: 15, of which 5 were waited for; matrix products, arithmetic and copies ran while one was open for 21% of the time, Pallas kernels for 0%

profile of v1, /device:TPU:32, one launch (start us, length us, event | category | flops | bytes accessed | tf_op | source)
XLA Modules:
  0.0 248.3 jit_solution(11255940481475490986)
XLA Ops:
  0.7 2.4 fusion.114
  5.2 1.9 copy-done
  7.0 1.5 fusion.113
  8.5 1.9 collective-permute-start
  10.5 9.6 %collective-permute-start.1 = (f32[7,1,64,256]{3,1,2,0:T(1,128)}, f32[7,1,64,256]{3,1,2,0:T(1,128)}, u32[]{:S(2)}, u32[]{:S(2)}) collective-permute-start(f32[7,1,64,256]{3,1,2,0:T(1,128)} %get-tuple-element.33), channel_id=1, source_target_pairs={{1,0},{2,1},{3,2},{4,3},{5,4},{6,5},{7,6},{8,7},{9,8},{10,9},{11,1... | collective-permute-start | bytes 1376264 | tf_op jit(solution)/shard_map/ppermute | solution.py:38
  21.5 5.8 %all-to-all-start = ((f32[8,1,2,8,256]{4,3,2,1,0:T(8,128)}), f32[8,1,2,8,256]{4,3,2,1,0:T(8,128)S(1)}, u32[]{:S(2)}, u32[]{:S(2)}) async-start(f32[8,1,2,8,256]{4,3,2,1,0:T(8,128)} %stack.55), calls=%async_computation | async-start | bytes 262144 | tf_op jit(solution)/shard_map/all_to_all | solution.py:20
  28.2 1.9 collective-permute-start.2
  30.2 8.8 %collective-permute-start.3 = (f32[1,64,256]{2,0,1:T(1,128)S(1)}, f32[1,64,256]{2,0,1:T(1,128)S(1)}, u32[]{:S(2)}, u32[]{:S(2)}) collective-permute-start(f32[1,64,256]{2,0,1:T(1,128)S(1)} %copy.125), channel_id=1, source_target_pairs={{1,0},{2,1},{3,2},{4,3},{5,4},{6,5},{7,6},{8,7},{9,8},{10,9},{11,1... | collective-permute-start | bytes 196616 | tf_op jit(solution)/shard_map/ppermute | solution.py:38
  41.6 1.7 fusion.137
  60.0 2.1 copy.306
  62.1 74.0 %psum.7 = f32[8]{0:T(128)S(1)} all-reduce(f32[8]{0:T(128)} %fusion.104), channel_id=1, replica_groups=mesh['zone'=8,'brick'=32] {'zone','brick'}, use_global_device_ids=true, to_apply=%region_3.4 | all-reduce | flops 8 | bytes 64 | tf_op jit(solution)/shard_map/psum | solution.py:156
  140.6 2.2 copy.299
  142.8 2.2 copy.300
  151.3 2.8 %fusion.61 = f32[8,64,256]{2,0,1:T(8,128)S(1)} fusion(f32[7,1,64,256]{3,1,2,0:T(1,128)} %collective-permute-done.1, f32[7,8,64,256]{3,1,2,0:T(8,128)} %copy-done, f32[7,1,64,256]{3,1,2,0:T(1,128)} %collective-permute-done, f32[8,64,255]{2,0,1:T(8,128)} %get-tuple-element.102, f32[8,64,255]{2,0,1:T(8,128)} %get-tuple-element.101, ...), kind=kLoop, calls=%fused_computation.82 | loop fusion | flops 1966080 | bytes 8757248 | tf_op jit(solution)/shard_map/add | solution.py:75
  156.7 4.4 %multiply_add_fusion = (f32[8,64,256]{2,0,1:T(8,128)S(1)}, f32[8,64,256]{2,0,1:T(8,128)S(1)}, f32[8,64,256]{2,0,1:T(8,128)S(1)}, f32[8,64,256]{2,0,1:T(8,128)S(1)}, f32[8,64,256]{2,0,1:T(8,128)S(1)}) fusion(f32[8,63,256]{2,0,1:T(8,128)S(1)} %copy-done.11, f32[8,63,256]{2,0,1:T(8,128)S(1)} %copy-done.12, f32[8,64,255]{2,0,1:T(8,128)S(1)} %copy.310, ...), kind=kLoop, calls=%fused_computation.137 | loop fusion | flops 7471104 | bytes 17094656 | tf_op jit(solution)/shard_map/add | solution.py:95
  162.8 3.2 %fusion.95 = (f32[8,64,256]{2,0,1:T(8,128)S(1)}, f32[8,64,256]{2,0,1:T(8,128)S(1)}) fusion(f32[8,64,256]{2,1,0:T(8,128)S(1)} %get-tuple-element.21, f32[8,64,255]{2,0,1:T(8,128)S(1)} %copy-done.18, f32[8,64,255]{2,0,1:T(8,128)S(1)} %copy-done.19, f32[8,63,256]{2,0,1:T(8,128)S(1)} %copy-done.30, f32[8,63,256]{2,0,1:T(8,128)S(1)} %copy-done.31, ...), kind=kLoop, calls=%fused_computation.134 | loop fusion | flops 5242880 | bytes 11382784 | tf_op jit(solution)/shard_map/sub | solution.py:150
  168.6 3.1 %collective-permute-start.4 = (f32[1,64,256]{2,0,1:T(1,128)S(1)}, f32[1,64,256]{2,0,1:T(1,128)S(1)}, u32[]{:S(2)}, u32[]{:S(2)}) collective-permute-start(f32[1,64,256]{2,0,1:T(1,128)S(1)} %get-tuple-element.73), channel_id=1, source_target_pairs={{1,0},{2,1},{3,2},{4,3},{5,4},{6,5},{7,6},{8,7},{9,8},{10,9},{11,1... | collective-permute-start | bytes 196616 | tf_op jit(solution)/shard_map/ppermute | solution.py:38
  171.7 2.1 collective-permute-start.5
  175.7 6.7 %collective-permute-done.5 = f32[1,64,256]{2,0,1:T(1,128)S(1)} collective-permute-done((f32[1,64,256]{2,0,1:T(1,128)S(1)}, f32[1,64,256]{2,0,1:T(1,128)S(1)}, u32[]{:S(2)}, u32[]{:S(2)}) %collective-permute-start.5) | collective-permute-done | bytes 65568 | tf_op jit(solution)/shard_map/ppermute | solution.py:36
  182.5 2.5 %fusion.46 = (f32[8,64,256]{2,0,1:T(8,128)S(1)}, f32[8,64,256]{2,0,1:T(8,128)S(1)}, f32[8,64,256]{2,0,1:T(8,128)S(1)}, f32[8,64,256]{2,0,1:T(8,128)S(1)}, f32[8,...) fusion(f32[1,64,256]{2,0,1:T(1,128)S(1)} %collective-permute-do, ...), kind=kLoop, calls=%fused_computation.63 | loop fusion | flops 5898240 | bytes 16977920 | tf_op jit(solution)/shard_map/jit(_where)/select_n | solution.py:121
  185.3 1.9 collective-permute-start.6
  187.2 8.8 %collective-permute-start.7 = (f32[1,64,256]{2,0,1:T(1,128)S(1)}, f32[1,64,256]{2,0,1:T(1,128)S(1)}, u32[]{:S(2)}, u32[]{:S(2)}) collective-permute-start(f32[1,64,256]{2,0,1:T(1,128)S(1)} %get-tuple-element.72), channel_id=1, source_target_pairs={{1,0},{2,1},{3,2},{4,3},{5,4},{6,5},{7,6},{8,7},{9,8},{10,9},{11,1... | collective-permute-start | bytes 196616 | tf_op jit(solution)/shard_map/ppermute | solution.py:38
  196.1 1.8 collective-permute-done.7
  198.9 1.9 collective-permute-start.8
  200.8 8.8 %collective-permute-start.9 = (f32[1,64,256]{2,0,1:T(1,128)S(1)}, f32[1,64,256]{2,0,1:T(1,128)S(1)}, u32[]{:S(2)}, u32[]{:S(2)}) collective-permute-start(f32[1,64,256]{2,0,1:T(1,128)S(1)} %get-tuple-element.66), channel_id=1, source_target_pairs={{1,0},{2,1},{3,2},{4,3},{5,4},{6,5},{7,6},{8,7},{9,8},{10,9},{11,1... | collective-permute-start | bytes 196616 | tf_op jit(solution)/shard_map/ppermute | solution.py:38
  209.7 1.8 collective-permute-done.9
  212.5 1.9 collective-permute-start.10
  214.4 8.8 %collective-permute-start.11 = (f32[1,64,256]{2,0,1:T(1,128)S(1)}, f32[1,64,256]{2,0,1:T(1,128)S(1)}, u32[]{:S(2)}, u32[]{:S(2)}) collective-permute-start(f32[1,64,256]{2,0,1:T(1,128)S(1)} %get-tuple-element.60), channel_id=1, source_target_pairs={{1,0},{2,1},{3,2},{4,3},{5,4},{6,5},{7,6},{8,7},{9,8},{10,9},{11,1... | collective-permute-start | bytes 196616 | tf_op jit(solution)/shard_map/ppermute | solution.py:38
  223.3 1.8 collective-permute-done.11
  226.8 8.8 %collective-permute-start.12 = (f32[1,64,256]{2,0,1:T(1,128)S(1)}, f32[1,64,256]{2,0,1:T(1,128)S(1)}, u32[]{:S(2)}, u32[]{:S(2)}) collective-permute-start(f32[1,64,256]{2,0,1:T(1,128)S(1)} %copy.140), channel_id=1, source_target_pairs={{1,0},{2,1},{3,2},{4,3},{5,4},{6,5},{7,6},{8,7},{9,8},{10,9},{11,1... | collective-permute-start | bytes 196616 | tf_op jit(solution)/shard_map/ppermute | solution.py:38
  235.7 1.9 collective-permute-start.13
  238.2 8.2 %collective-permute-done.13 = f32[1,64,256]{2,0,1:T(1,128)S(1)} collective-permute-done((f32[1,64,256]{2,0,1:T(1,128)S(1)}, f32[1,64,256]{2,0,1:T(1,128)S(1)}, u32[]{:S(2)}, u32[]{:S(2)}) %collective-permute-start.13) | collective-permute-done | bytes 65568 | tf_op jit(solution)/shard_map/ppermute | solution.py:36
  (177 shorter events, 45.1 us)
Async XLA Ops:
  3.1 35.9 %copy-start.5 = (f32[3,8,64,256]{3,1,2,0:T(8,128)}, f32[3,8,64,256]{3,1,2,0:T(8,128)S(1)}, u32[]{:S(2)}) copy-start(f32[3,8,64,256]{3,1,2,0:T(8,128)S(1)} %get-tuple-element.37) | copy-start | bytes 4718596
  8.5 142.6 %collective-permute-start = (f32[7,1,64,256]{3,1,2,0:T(1,128)}, f32[7,1,64,256]{3,1,2,0:T(1,128)}, u32[]{:S(2)}, u32[]{:S(2)}) collective-permute-start(f32[7,1,64,256]{3,1,2,0:T(1,128)} %get-tuple-element.32), channel_id=1, source_target_pairs={{0,1},{1,2},{2,3},{3,4},{4,5},{5,6},{6,7},{7,8},{8,9},{9,10},{10,1... | collective-permute-start | bytes 1376264 | tf_op jit(solution)/shard_map/ppermute | solution.py:36
  10.5 140.7 %collective-permute-start.1 = (f32[7,1,64,256]{3,1,2,0:T(1,128)}, f32[7,1,64,256]{3,1,2,0:T(1,128)}, u32[]{:S(2)}, u32[]{:S(2)}) collective-permute-start(f32[7,1,64,256]{3,1,2,0:T(1,128)} %get-tuple-element.33), channel_id=1, source_target_pairs={{1,0},{2,1},{3,2},{4,3},{5,4},{6,5},{7,6},{8,7},{9,8},{10,9},{11,1... | collective-permute-start | bytes 1376264 | tf_op jit(solution)/shard_map/ppermute | solution.py:38
  21.5 129.6 %all-to-all-start = ((f32[8,1,2,8,256]{4,3,2,1,0:T(8,128)}), f32[8,1,2,8,256]{4,3,2,1,0:T(8,128)S(1)}, u32[]{:S(2)}, u32[]{:S(2)}) async-start(f32[8,1,2,8,256]{4,3,2,1,0:T(8,128)} %stack.55), calls=%async_computation | async-start | bytes 262144 | tf_op jit(solution)/shard_map/all_to_all | solution.py:20
  28.2 147.6 %collective-permute-start.2 = (f32[1,64,256]{2,0,1:T(1,128)S(1)}, f32[1,64,256]{2,0,1:T(1,128)S(1)}, u32[]{:S(2)}, u32[]{:S(2)}) collective-permute-start(f32[1,64,256]{2,0,1:T(1,128)S(1)} %copy.122), channel_id=1, source_target_pairs={{0,1},{1,2},{2,3},{3,4},{4,5},{5,6},{6,7},{7,8},{8,9},{9,10},{10,1... | collective-permute-start | bytes 196616 | tf_op jit(solution)/shard_map/ppermute | solution.py:36
  30.2 145.6 %collective-permute-start.3 = (f32[1,64,256]{2,0,1:T(1,128)S(1)}, f32[1,64,256]{2,0,1:T(1,128)S(1)}, u32[]{:S(2)}, u32[]{:S(2)}) collective-permute-start(f32[1,64,256]{2,0,1:T(1,128)S(1)} %copy.125), channel_id=1, source_target_pairs={{1,0},{2,1},{3,2},{4,3},{5,4},{6,5},{7,6},{8,7},{9,8},{10,9},{11,1... | collective-permute-start | bytes 196616 | tf_op jit(solution)/shard_map/ppermute | solution.py:38
  55.1 82.2 %copy-start.37 = (s32[1,2]{1,0:T(1,128)S(1)}, s32[1,2]{1,0:T(1,128)}, u32[]{:S(2)}) copy-start(s32[1,2]{1,0:T(1,128)} %param.21) | copy-start | bytes 28
  55.1 82.8 %copy-start.39 = (f32[8]{0:T(128)S(1)}, f32[8]{0:T(128)}, u32[]{:S(2)}) copy-start(f32[8]{0:T(128)} %param.19) | copy-start | bytes 100
  140.6 4.5 %copy-start.23 = (f32[8,63,256]{2,1,0:T(8,128)S(1)}, f32[8,63,256]{2,1,0:T(8,128)}, u32[]{:S(2)}) copy-start(f32[8,63,256]{2,1,0:T(8,128)} %get-tuple-element.81) | copy-start | bytes 1548292
  140.6 5.5 %copy-start.22 = (f32[8,63,256]{2,1,0:T(8,128)S(1)}, f32[8,63,256]{2,1,0:T(8,128)}, u32[]{:S(2)}) copy-start(f32[8,63,256]{2,1,0:T(8,128)} %get-tuple-element.82) | copy-start | bytes 1548292
  142.8 4.4 %copy-start.21 = (f32[8,64,256]{2,0,1:T(8,128)S(1)}, f32[8,64,256]{2,0,1:T(8,128)}, u32[]{:S(2)}) copy-start(f32[8,64,256]{2,0,1:T(8,128)} %broadcast_multiply_fusion) | copy-start | bytes 1572868
  151.3 4.2 %copy-start.26 = (f32[8,64,255]{2,0,1:T(8,128)S(1)}, f32[8,64,255]{2,0,1:T(8,128)}, u32[]{:S(2)}) copy-start(f32[8,64,255]{2,0,1:T(8,128)} %get-tuple-element.107) | copy-start | bytes 1566724
  151.3 4.4 %copy-start.27 = (f32[8,64,255]{2,0,1:T(8,128)S(1)}, f32[8,64,255]{2,0,1:T(8,128)}, u32[]{:S(2)}) copy-start(f32[8,64,255]{2,0,1:T(8,128)} %get-tuple-element.108) | copy-start | bytes 1566724
  151.3 4.5 %copy-start.32 = (f32[8,63,256]{2,0,1:T(8,128)S(1)}, f32[8,63,256]{2,0,1:T(8,128)}, u32[]{:S(2)}) copy-start(f32[8,63,256]{2,0,1:T(8,128)} %get-tuple-element.85) | copy-start | bytes 1548292
  151.3 4.6 %copy-start.33 = (f32[8,63,256]{2,0,1:T(8,128)S(1)}, f32[8,63,256]{2,0,1:T(8,128)}, u32[]{:S(2)}) copy-start(f32[8,63,256]{2,0,1:T(8,128)} %get-tuple-element.86) | copy-start | bytes 1548292
  156.7 4.4 %copy-start.20 = (f32[8,64,255]{2,0,1:T(8,128)S(1)}, f32[8,64,255]{2,0,1:T(8,128)}, u32[]{:S(2)}) copy-start(f32[8,64,255]{2,0,1:T(8,128)} %copy.309) | copy-start | bytes 1566724
  168.6 7.1 %collective-permute-start.4 = (f32[1,64,256]{2,0,1:T(1,128)S(1)}, f32[1,64,256]{2,0,1:T(1,128)S(1)}, u32[]{:S(2)}, u32[]{:S(2)}) collective-permute-start(f32[1,64,256]{2,0,1:T(1,128)S(1)} %get-tuple-element.73), channel_id=1, source_target_pairs={{1,0},{2,1},{3,2},{4,3},{5,4},{6,5},{7,6},{8,7},{9,8},{10,9},{11,1... | collective-permute-start | bytes 196616 | tf_op jit(solution)/shard_map/ppermute | solution.py:38
  171.7 10.8 %collective-permute-start.5 = (f32[1,64,256]{2,0,1:T(1,128)S(1)}, f32[1,64,256]{2,0,1:T(1,128)S(1)}, u32[]{:S(2)}, u32[]{:S(2)}) collective-permute-start(f32[1,64,256]{2,0,1:T(1,128)S(1)} %get-tuple-element.74), channel_id=1, source_target_pairs={{0,1},{1,2},{2,3},{3,4},{4,5},{5,6},{6,7},{7,8},{8,9},{9,10},{10,1... | collective-permute-start | bytes 196616 | tf_op jit(solution)/shard_map/ppermute | solution.py:36
  174.5 8.0 %copy-start.8 = (f32[8,64,255]{2,0,1:T(8,128)S(1)}, f32[8,64,255]{2,0,1:T(8,128)}, u32[]{:S(2)}) copy-start(f32[8,64,255]{2,0,1:T(8,128)} %get-tuple-element.98) | copy-start | bytes 1566724
  174.5 8.0 %copy-start.16 = (f32[8,64,255]{2,0,1:T(8,128)S(1)}, f32[8,64,255]{2,0,1:T(8,128)}, u32[]{:S(2)}) copy-start(f32[8,64,255]{2,0,1:T(8,128)} %copy.299) | copy-start | bytes 1566724
  174.5 8.0 %copy-start.17 = (f32[8,64,255]{2,0,1:T(8,128)S(1)}, f32[8,64,255]{2,0,1:T(8,128)}, u32[]{:S(2)}) copy-start(f32[8,64,255]{2,0,1:T(8,128)} %copy.300) | copy-start | bytes 1566724
  174.5 8.0 %copy-start.28 = (f32[8,63,256]{2,0,1:T(8,128)S(1)}, f32[8,63,256]{2,0,1:T(8,128)}, u32[]{:S(2)}) copy-start(f32[8,63,256]{2,0,1:T(8,128)} %copy.301) | copy-start | bytes 1548292
  174.5 8.0 %copy-start.29 = (f32[8,63,256]{2,0,1:T(8,128)S(1)}, f32[8,63,256]{2,0,1:T(8,128)}, u32[]{:S(2)}) copy-start(f32[8,63,256]{2,0,1:T(8,128)} %copy.302) | copy-start | bytes 1548292
  185.3 10.8 %collective-permute-start.6 = (f32[1,64,256]{2,0,1:T(1,128)S(1)}, f32[1,64,256]{2,0,1:T(1,128)S(1)}, u32[]{:S(2)}, u32[]{:S(2)}) collective-permute-start(f32[1,64,256]{2,0,1:T(1,128)S(1)} %get-tuple-element.71), channel_id=1, source_target_pairs={{0,1},{1,2},{2,3},{3,4},{4,5},{5,6},{6,7},{7,8},{8,9},{9,10},{10,1... | collective-permute-start | bytes 196616 | tf_op jit(solution)/shard_map/ppermute | solution.py:36
  187.2 10.7 %collective-permute-start.7 = (f32[1,64,256]{2,0,1:T(1,128)S(1)}, f32[1,64,256]{2,0,1:T(1,128)S(1)}, u32[]{:S(2)}, u32[]{:S(2)}) collective-permute-start(f32[1,64,256]{2,0,1:T(1,128)S(1)} %get-tuple-element.72), channel_id=1, source_target_pairs={{1,0},{2,1},{3,2},{4,3},{5,4},{6,5},{7,6},{8,7},{9,8},{10,9},{11,1... | collective-permute-start | bytes 196616 | tf_op jit(solution)/shard_map/ppermute | solution.py:38
  198.9 10.8 %collective-permute-start.8 = (f32[1,64,256]{2,0,1:T(1,128)S(1)}, f32[1,64,256]{2,0,1:T(1,128)S(1)}, u32[]{:S(2)}, u32[]{:S(2)}) collective-permute-start(f32[1,64,256]{2,0,1:T(1,128)S(1)} %get-tuple-element.65), channel_id=1, source_target_pairs={{0,1},{1,2},{2,3},{3,4},{4,5},{5,6},{6,7},{7,8},{8,9},{9,10},{10,1... | collective-permute-start | bytes 196616 | tf_op jit(solution)/shard_map/ppermute | solution.py:36
  200.8 10.7 %collective-permute-start.9 = (f32[1,64,256]{2,0,1:T(1,128)S(1)}, f32[1,64,256]{2,0,1:T(1,128)S(1)}, u32[]{:S(2)}, u32[]{:S(2)}) collective-permute-start(f32[1,64,256]{2,0,1:T(1,128)S(1)} %get-tuple-element.66), channel_id=1, source_target_pairs={{1,0},{2,1},{3,2},{4,3},{5,4},{6,5},{7,6},{8,7},{9,8},{10,9},{11,1... | collective-permute-start | bytes 196616 | tf_op jit(solution)/shard_map/ppermute | solution.py:38
  212.5 10.8 %collective-permute-start.10 = (f32[1,64,256]{2,0,1:T(1,128)S(1)}, f32[1,64,256]{2,0,1:T(1,128)S(1)}, u32[]{:S(2)}, u32[]{:S(2)}) collective-permute-start(f32[1,64,256]{2,0,1:T(1,128)S(1)} %get-tuple-element.59), channel_id=1, source_target_pairs={{0,1},{1,2},{2,3},{3,4},{4,5},{5,6},{6,7},{7,8},{8,9},{9,10},{10,1... | collective-permute-start | bytes 196616 | tf_op jit(solution)/shard_map/ppermute | solution.py:36
  214.4 10.7 %collective-permute-start.11 = (f32[1,64,256]{2,0,1:T(1,128)S(1)}, f32[1,64,256]{2,0,1:T(1,128)S(1)}, u32[]{:S(2)}, u32[]{:S(2)}) collective-permute-start(f32[1,64,256]{2,0,1:T(1,128)S(1)} %get-tuple-element.60), channel_id=1, source_target_pairs={{1,0},{2,1},{3,2},{4,3},{5,4},{6,5},{7,6},{8,7},{9,8},{10,9},{11,1... | collective-permute-start | bytes 196616 | tf_op jit(solution)/shard_map/ppermute | solution.py:38
  226.8 11.4 %collective-permute-start.12 = (f32[1,64,256]{2,0,1:T(1,128)S(1)}, f32[1,64,256]{2,0,1:T(1,128)S(1)}, u32[]{:S(2)}, u32[]{:S(2)}) collective-permute-start(f32[1,64,256]{2,0,1:T(1,128)S(1)} %copy.140), channel_id=1, source_target_pairs={{1,0},{2,1},{3,2},{4,3},{5,4},{6,5},{7,6},{8,7},{9,8},{10,9},{11,1... | collective-permute-start | bytes 196616 | tf_op jit(solution)/shard_map/ppermute | solution.py:38
  235.7 10.7 %collective-permute-start.13 = (f32[1,64,256]{2,0,1:T(1,128)S(1)}, f32[1,64,256]{2,0,1:T(1,128)S(1)}, u32[]{:S(2)}, u32[]{:S(2)}) collective-permute-start(f32[1,64,256]{2,0,1:T(1,128)S(1)} %copy.142), channel_id=1, source_target_pairs={{0,1},{1,2},{2,3},{3,4},{4,5},{5,6},{6,7},{7,8},{8,9},{9,10},{10,1... | collective-permute-start | bytes 196616 | tf_op jit(solution)/shard_map/ppermute | solution.py:36
  238.0 8.8 %copy-start.15 = (f32[8,64,256]{2,1,0:T(8,128)S(1)}, f32[8,64,256]{2,1,0:T(8,128)}, u32[]{:S(2)}) copy-start(f32[8,64,256]{2,1,0:T(8,128)} %copy.119) | copy-start | bytes 1572868
  (23 other events, 54.7 us)
